TPU v7x, 256 devices: a whole 4x4x8 slice. The times are simulated.
256 devices in a mesh: walker: 2 (over core), grp: 128 (over z, x, y).
Axes of the slice: x: 4, y: 4, z: 8, core: 2. Of those that a mesh axis runs over, the one named last changes fastest.
Arguments:
- feats: bfloat16 [4096, 256], P(('walker', 'grp')), parts along dimension 0, may hold values from -6 to 6
- perm: int32 [4096], P('walker'), parts along dimension 0, may hold values from 0 to 2047, each once
- w_left: bfloat16 [256, 256], replicated, may hold values from -0.375 to 0.375
- w_right: bfloat16 [256, 256], replicated, may hold values from -0.375 to 0.375
- bias_in: float32 [256], replicated, may hold values from -3 to 3
- w_hidden: bfloat16 [256, 256], replicated, may hold values from -0.375 to 0.375
- bias_hidden: float32 [256], replicated, may hold values from -3 to 3
- w_out: float32 [256], replicated, may hold values from -0.375 to 0.375
- pair_strength: float32 [128], replicated, may hold values from 16 to 32
Outputs:
- log_pivot: float32 [256], P('walker'), parts along dimension 0
- panel_cols: float32 [3584, 256], P(('walker', 'grp')), parts along dimension 0
- schur: float32 [3584, 1792], P(('walker', 'grp')), parts along dimension 0
There are 2 independent parts, one for each index of `walker`. A program takes and returns all parts, laid end to end along the dimension named above; an argument that names none is the same for every part. Nothing has to cross between parts.
Inputs may be any that keep to these rules, and one draw needn't show every extreme that they name: `perm`: each position 0 to 2047 appears exactly once.
All inputs are finite; a program needn't handle non-finite values.
Results may differ from a plain program's by a relative error of at most 0.0062.
Values may be sent and summed in bfloat16 or wider, within the bound.
No kernel may reach another device: no remote copies, remote signals or barrier semaphores. Data moves between devices by JAX's collectives and lax.ppermute only.
A program may use at most 64 MiB of HBM per device.

v0:
```python
import jax
import jax.numpy as jnp
from jax import lax
from jax.sharding import PartitionSpec as P


def orbitals(left_part, right_part, bias_in, w_hidden, bias_hidden, w_out):
    pre = (
        left_part.astype(jnp.float32)[:, None, :]
        + right_part.astype(jnp.float32)[None, :, :]
        + bias_in
    )
    gated = jax.nn.silu(pre).astype(jnp.bfloat16).reshape(-1, pre.shape[-1])
    hidden = jax.nn.silu(jnp.dot(gated, w_hidden, preferred_element_type=jnp.float32) + bias_hidden)
    values = jnp.dot(hidden, w_out, precision=lax.Precision.HIGHEST)
    return values.reshape(left_part.shape[0], right_part.shape[0])


def column_width():
    return 128


def forward_terms(left_rows, right_cols, params):
    count = right_cols.shape[0]
    width = column_width()
    pieces = right_cols.reshape(count // width, width, right_cols.shape[1])
    result = lax.map(lambda piece: orbitals(left_rows, piece, *params), pieces)
    return jnp.transpose(result, (1, 0, 2)).reshape(left_rows.shape[0], count)


def backward_terms(right_rows, left_cols, params):
    count = left_cols.shape[0]
    width = column_width()
    pieces = left_cols.reshape(count // width, width, left_cols.shape[1])
    result = lax.map(lambda piece: orbitals(piece, right_rows, *params), pieces)
    return result.reshape(count, right_rows.shape[0]).T


def factor_block(block):
    size = block.shape[0]
    position = jnp.arange(size)

    def advance(step, carry):
        matrix, lower, pivots = carry
        first = (2 * step).astype(jnp.int32)
        col_even = lax.dynamic_slice_in_dim(matrix, first, 1, 1)[:, 0]
        col_odd = lax.dynamic_slice_in_dim(matrix, first + 1, 1, 1)[:, 0]
        pivot = lax.dynamic_index_in_dim(col_odd, first, 0, keepdims=False)
        keep = position >= first
        zeros = jnp.zeros_like(col_even)
        lower_even = jnp.where(keep, col_odd / pivot, zeros)
        lower_odd = jnp.where(keep, -col_even / pivot, zeros)
        lower = lax.dynamic_update_slice(
            lower, jnp.stack([lower_even, lower_odd], axis=1), (jnp.int32(0), first)
        )
        rest = position > first + 1
        keep_even = jnp.where(rest, col_even, zeros)
        keep_odd = jnp.where(rest, col_odd, zeros)
        matrix = (
            matrix
            + (keep_odd[:, None] * keep_even[None, :] - keep_even[:, None] * keep_odd[None, :])
            / pivot
        )
        pivots = lax.dynamic_update_slice(pivots, pivot[None], (step.astype(jnp.int32),))
        return (matrix, lower, pivots)

    start = (block, jnp.zeros_like(block), jnp.zeros((size // 2,), block.dtype))
    matrix, lower, pivots = lax.fori_loop(0, size // 2, advance, start)
    return (lower, pivots)


def pair_scale(columns, pivots):
    count = columns.shape[0]
    grouped = columns.reshape(count, -1, 2)
    swapped = jnp.stack([grouped[:, :, 1], -grouped[:, :, 0]], axis=2).reshape(count, -1)
    return swapped / jnp.repeat(pivots, 2)[None, :]


def solve_rows(lower, rows):
    return jax.scipy.linalg.solve_triangular(lower, rows.T, lower=True, unit_diagonal=True).T


def on_device(feats, perm, w_left, w_right, bias_in, w_hidden, bias_hidden, w_out, pair_strength):
    groups = lax.axis_size("grp")
    device = lax.axis_index("grp")
    electrons = perm.shape[0]
    panel = 2 * pair_strength.shape[0]
    share = panel // groups
    tail = (electrons - panel) // groups
    params = (bias_in, w_hidden, bias_hidden, w_out)
    left_own = jnp.dot(feats, w_left, preferred_element_type=jnp.float32).astype(jnp.bfloat16)
    right_own = jnp.dot(feats, w_right, preferred_element_type=jnp.float32).astype(jnp.bfloat16)
    left_every, right_every = (
        lax.all_gather(left_own, "grp", axis=0, tiled=True),
        lax.all_gather(right_own, "grp", axis=0, tiled=True),
    )
    left_all = jnp.take(left_every, perm, axis=0)
    right_all = jnp.take(right_every, perm, axis=0)
    top_start = device * share
    tail_start = panel + device * tail
    left_rows = jnp.concatenate(
        [
            lax.dynamic_slice_in_dim(left_all, top_start, share, 0),
            lax.dynamic_slice_in_dim(left_all, tail_start, tail, 0),
        ],
        axis=0,
    )
    right_rows = jnp.concatenate(
        [
            lax.dynamic_slice_in_dim(right_all, top_start, share, 0),
            lax.dynamic_slice_in_dim(right_all, tail_start, tail, 0),
        ],
        axis=0,
    )
    top_rows = forward_terms(left_rows[:share], right_all[:panel], params) - backward_terms(
        right_rows[:share], left_all[:panel], params
    )
    tail_rows = forward_terms(left_rows[share:], right_all, params) - backward_terms(
        right_rows[share:], left_all, params
    )
    block_rows = lax.all_gather(top_rows, "grp", axis=0, tiled=True)
    pattern = jnp.array([[0.0, 1.0], [-1.0, 0.0]], dtype=pair_strength.dtype)
    block = block_rows + jnp.kron(jnp.diag(pair_strength), pattern)
    lower, pivots = factor_block(block)
    log_pivot = jnp.log(jnp.abs(pivots))
    below_own = tail_rows[:, :panel]
    trailing_own = tail_rows[:, panel:]
    panel_own = solve_rows(lower, below_own)
    scaled_own = pair_scale(panel_own, pivots)
    schur = trailing_own - jnp.dot(
        panel_own,
        lax.all_gather(scaled_own, "grp", axis=0, tiled=True).T,
        precision=lax.Precision.HIGHEST,
    )
    return (log_pivot, panel_own, schur)


def solution(mesh):
    return jax.shard_map(
        on_device,
        mesh=mesh,
        in_specs=(P(("walker", "grp"), None), P("walker"), P(), P(), P(), P(), P(), P(), P()),
        out_specs=(P("walker"), P(("walker", "grp"), None), P(("walker", "grp"), None)),
        check_vma=False,
    )
```

profile of v0, /device:TPU:6, one launch (start us, length us, event | category | flops | bytes accessed | tf_op | source)
XLA Modules:
  0.0 1272.6 jit_solution(9753338062024064957)
XLA Ops:
  12.1 7.3 broadcast_multiply_fusion
  19.5 13.2 %mul.191 = f32[256,256]{1,0:T(8,128)} reshape(f32[128,2,128,2]{3,2,1,0:T(8,128)} %broadcast_multiply_fusion) | data formatting | bytes 524288 | tf_op jit(solution)/shard_map/jit(kron)/mul | solution.py:123
  33.8 83.8 %all-gather.6.cloned.1.call-done = bf16[2048,256]{1,0:T(8,128)(2,1)} async-done(((bf16[16,256]{1,0:T(8,128)(2,1)}), bf16[2048,256]{1,0:T(8,128)(2,1)}) %all-gather.6.cloned.1.call-update) | async-done | bytes 1048592 | tf_op jit(solution)/shard_map/all_gather | solution.py:94
  117.5 8.0 gather_fusion
  125.5 97.7 %all-gather.8.cloned.1.call-done = bf16[2048,256]{1,0:T(8,128)(2,1)} async-done(((bf16[16,256]{1,0:T(8,128)(2,1)}), bf16[2048,256]{1,0:T(8,128)(2,1)}) %all-gather.8.cloned.1.call-update) | async-done | bytes 1048592 | tf_op jit(solution)/shard_map/all_gather | solution.py:95
  223.2 8.0 gather_fusion.1
  234.8 64.1 %while.65 = (s32[]{:T(128)}, f32[16,14,128]{2,1,0:T(8,128)S(1)}, bf16[14,256]{1,0:T(8,128)(2,1)S(1)}, bf16[16,128,256]{2,1,0:T(8,128)(2,1)}, f32[256]{0:T(256)S(...) while((s32[]{:T(128)}, f32[16,14,128]{2,1,0:T(8,128)S(1)}, ...), condition=%wide.region_7.9_spmd, body=%wide.region_6.8_spmd.sunk | while | flops 245927424 | bytes 9696365 | solution.py:27
  240.8 2.0 fusion.106
  299.6 2.5 while.64
  302.2 315.5 %all-gather = f32[128,2,256]{2,1,0:T(2,128)S(1)} all-gather(f32[1,2,256]{2,1,0:T(2,128)S(1)} %fusion.53), channel_id=1, replica_groups=mesh['walker'=2,'grp'=128] {'grp'}, dimensions={0}, use_global_device_ids=true | all-gather | bytes 264192 | tf_op jit(solution)/shard_map/all_gather | solution.py:121
  618.5 107.8 %while.66 = (s32[]{:T(128)}, f32[16,128,14]{2,1,0:T(8,128)}, bf16[16,128,256]{2,1,0:T(8,128)(2,1)S(1)}, bf16[14,256]{1,0:T(8,128)(2,1)S(1)}, f32[256]{0:T(256)S(...) while((s32[]{:T(128)}, f32[16,128,14]{2,1,0:T(8,128)}, ...), condition=%wide.region_9.11_spmd, body=%wide.region_8.10_spmd.sunk | while | flops 245927424 | bytes 11606153 | solution.py:35
  620.3 2.1 convolution_add_fusion.11
  622.5 2.0 fusion.110
  627.1 2.1 convolution_add_fusion.11
  629.2 2.0 fusion.110
  633.8 2.1 convolution_add_fusion.11
  636.0 2.0 fusion.110
  640.5 2.1 convolution_add_fusion.11
  642.7 2.0 fusion.110
  647.3 2.1 convolution_add_fusion.11
  649.4 2.0 fusion.110
  654.0 2.1 convolution_add_fusion.11
  656.2 2.0 fusion.110
  660.8 2.1 convolution_add_fusion.11
  662.9 2.0 fusion.110
  667.5 2.1 convolution_add_fusion.11
  669.7 2.0 fusion.110
  674.2 2.1 convolution_add_fusion.11
  676.4 2.0 fusion.110
  681.0 2.1 convolution_add_fusion.11
  683.1 2.0 fusion.110
  687.7 2.1 convolution_add_fusion.11
  689.9 2.0 fusion.110
  694.5 2.1 convolution_add_fusion.11
  696.6 2.0 fusion.110
  701.2 2.1 convolution_add_fusion.11
  703.3 2.0 fusion.110
  707.9 2.1 convolution_add_fusion.11
  710.1 2.0 fusion.110
  714.7 2.1 convolution_add_fusion.11
  716.8 2.0 fusion.110
  721.4 2.1 convolution_add_fusion.11
  723.6 2.0 fusion.110
  729.2 365.8 %while.68 = (s32[]{:T(128)}, f32[256,256]{0,1:T(8,128)S(1)}, f32[256,256]{0,1:T(8,128)S(1)}, f32[128]{0:T(128)S(1)}, s32[]{:T(128)}, /*index=5*/s32[]{:T(128)}, s32[]{:T(128)}, s32[]{:T(128)}, s32[]{:T(128)}, s32[]{:T(128)}) while((s32[]{:T(128)}, f32[256,256]{0,1:T(8,128)S(1)}, f32[256,256]{0,1:T(8,128)S(1)}, ...), condition=%wide.region_5.7_spmd.clone.clone, body=%wide.region_4.6_spmd.clone.clone.sunk | while | flops 331276 | bytes 548637 | solution.py:68
  1095.1 5.4 while.67
  1100.6 20.5 %custom-call.4 = f32[2,128,128]{1,2,0:T(8,128)S(1)} custom-call(f32[2,128,128]{2,1,0:T(8,128)} %get-tuple-element.340), custom_call_target="InvertDiagBlocksLowerTriangular" | custom-call | tf_op jit(solution)/shard_map/jit(_solve_triangular)/triangular_solve | solution.py:80
  1123.5 138.6 %all-gather.10.cloned.1.call-done = f32[128,14,256]{2,1,0:T(8,128)} async-done(((f32[1,14,256]{2,1,0:T(8,128)}), f32[128,14,256]{2,1,0:T(8,128)}) %all-gather.10.cloned.1.call-update) | async-done | bytes 1835024 | tf_op jit(solution)/shard_map/all_gather | solution.py:132
  1263.8 2.3 convolution_subtract_fusion
  (1519 shorter events, 484.2 us)
Async XLA Ops:
  7.2 0.9 copy-start
  7.2 110.4 %all-gather.6.cloned.1.call-start = ((), (), s32[]{:S(2)}) async-start(), calls=%async_computation | async-start | bytes 1056768 | tf_op jit(solution)/shard_map/all_gather | solution.py:94
  9.5 213.7 %all-gather.8.cloned.1.call-start = ((), (), s32[]{:S(2)}) async-start(), calls=%async_computation.1 | async-start | bytes 1056768 | tf_op jit(solution)/shard_map/all_gather | solution.py:95
  11.3 1250.9 %all-gather.10.cloned.1.call-start = ((), (), s32[]{:S(2)}) async-start(), calls=%async_computation.2 | async-start | bytes 2113536 | tf_op jit(solution)/shard_map/all_gather | solution.py:132
  19.4 14.3 %copy-start.8 = (s32[2048]{0:T(1024)S(1)}, s32[2048]{0:T(1024)}, u32[]{:S(2)}) copy-start(s32[2048]{0:T(1024)} %param.23) | copy-start | bytes 24580
  231.2 1.5 copy-start.1
  231.2 1.5 copy-start.5
  231.2 1.5 copy-start.6
  231.3 1.5 copy-start.13
  231.7 1.0 copy-start.2
  232.8 1.5 copy-start.4
  234.2 0.6 copy-start.9
  234.3 65.3 %copy-start.3 = (f32[2,128,2]{2,1,0:T(8,128)S(1)}, f32[2,128,2]{2,1,0:T(8,128)}, u32[]{:S(2)}) copy-start(f32[2,128,2]{2,1,0:T(8,128)} %custom-call.10) | copy-start | bytes 6148
  299.0 0.6 copy-start.14
  299.6 2.6 copy-start.10
  299.6 0.7 copy-start.15
  300.8 0.7 copy-start.15
  620.3 2.1 copy-start.16
  627.1 2.1 copy-start.16
  633.8 2.1 copy-start.16
  640.5 2.1 copy-start.16
  647.3 2.1 copy-start.16
  654.0 2.1 copy-start.16
  660.8 2.1 copy-start.16
  667.5 2.1 copy-start.16
  674.2 2.1 copy-start.16
  681.0 2.1 copy-start.16
  687.7 2.1 copy-start.16
  694.5 2.1 copy-start.16
  701.2 2.1 copy-start.16
  707.9 2.1 copy-start.16
  714.7 2.1 copy-start.16
  721.4 2.1 copy-start.16
  726.3 2.8 copy-start.12
  729.1 365.9 %copy-start.11 = (s32[256]{0:T(256)S(1)}, s32[256]{0:T(256)}, u32[]{:S(2)}) copy-start(s32[256]{0:T(256)} %iota_add_fusion) | copy-start | bytes 3076
  729.2 365.9 %copy-start.17 = (s32[2]{0:T(128)S(1)}, s32[2]{0:T(128)}, u32[]{:S(2)}) copy-start(s32[2]{0:T(128)} %iota_multiply_fusion) | copy-start | bytes 28
  1121.6 142.3 %copy-start.7 = (f32[14,256]{1,0:T(8,128)}, f32[14,256]{1,0:T(8,128)S(1)}, u32[]{:S(2)}) copy-start(f32[14,256]{1,0:T(8,128)S(1)} %fusion.50) | copy-start | bytes 43012
Sparse Core Ops, SparseCore 0:
  12.0 105.5 all-gather.5
  121.5 101.6 all-gather.7
  1123.1 138.9 all-gather.9
where the time goes:
time: 1280 us; the launch traced here: 1270 us
  waiting for transfers between devices  320 us (25%)
  blocking collectives  315 us (25%)
  other arithmetic  256 us (20%)
  local copies, waits for them, and re-layouts  242 us (19%)
  matrix products  113 us (9%)
  between operations  14.3 us (1%)
    all_gather x1, blocking collectives, on_device(): block_rows = lax.all_gather(top_rows, 'grp', axis=0, tiled=True)  315 us
    all_gather x1, waiting for transfers between devices, on_device(): lax.all_gather(scaled_own, 'grp', axis=0, tiled=True)  139 us
    add x128, other arithmetic, advance(): matrix + (keep_odd[:, None] * keep_even[None, :] - keep_even[:, None] * k...  104 us
    all_gather x1, waiting for transfers between devices, on_device(): lax.all_gather(right_own, 'grp', axis=0, tiled=True)  97.7 us
    dynamic_update_slice x128, local copies, waits for them, and re-layouts, advance(): lax.dynamic_update_slice(pivots, pivot[None], (step.astype(jnp.int32),))  86.2 us
    select_n x128, other arithmetic, advance(): lower_odd = jnp.where(keep, -col_even / pivot, zeros)  84.3 us
    all_gather x1, waiting for transfers between devices, on_device(): lax.all_gather(left_own, 'grp', axis=0, tiled=True)  83.8 us
    dynamic_slice x128, local copies, waits for them, and re-layouts, advance(): pivot = lax.dynamic_index_in_dim(col_odd, first, 0, keepdims=False)  75.5 us
  transfers between devices with their start and end apart: 3, of which 3 were waited for; matrix products, arithmetic and copies ran while one was open for 3% of the time, Pallas kernels for 0%

commit v1 on v0

--- a/solution.py
+++ b/solution.py
@@ -91,7 +91,9 @@
     left_own = jnp.dot(feats, w_left, preferred_element_type=jnp.float32).astype(jnp.bfloat16)
     right_own = jnp.dot(feats, w_right, preferred_element_type=jnp.float32).astype(jnp.bfloat16)
     left_every, right_every = (
-        lax.all_gather(left_own, "grp", axis=0, tiled=True),
+        jnp.concatenate(
+            lax.all_to_all(jnp.stack([left_own] * lax.axis_size("grp")), "grp", 0, 0), axis=0
+        ),
         lax.all_gather(right_own, "grp", axis=0, tiled=True),
     )
     left_all = jnp.take(left_every, perm, axis=0)

time: 1280 us -> 1190 us (0.930)
  waiting for transfers between devices: 320 us -> 209 us
  starting transfers between devices: 0.12 us -> 15.5 us
  local copies, waits for them, and re-layouts: 242 us -> 255 us
    all_gather x1 -> x0, waiting for transfers between devices: 83.8 us -> none  [on_device(): lax.all_gather(left_own, 'grp', axis=0, tiled=True)]
    all_gather x1, waiting for transfers between devices: 97.7 us -> 69.9 us  [on_device(): lax.all_gather(right_own, 'grp', axis=0, tiled=True)]
    all_to_all x0 -> x1, starting transfers between devices: none -> 15.4 us  [on_device(): lax.all_to_all(jnp.stack([left_own] * lax.axis_size('grp')), 'grp', 0, 0)]
    add x54, other arithmetic: 21.4 us -> 7.84 us  [orbitals(): left_part.astype(jnp.float32)[:, None, :]]
    convert_element_type x36, other arithmetic: 0.31 us -> 13.7 us  [orbitals(): left_part.astype(jnp.float32)[:, None, :]]
  transfers between devices with their start and end apart: 3 -> 3, of which waited for: 3 -> 2; matrix products, arithmetic and copies ran while one was open for 3% -> 3% of each run, Pallas kernels for 0% -> 0%
where the time goes in v1:
time: 1190 us
  blocking collectives  315 us (26%)
  local copies, waits for them, and re-layouts  255 us (21%)
  other arithmetic  253 us (21%)
  waiting for transfers between devices  209 us (18%)
  matrix products  113 us (9%)
  starting transfers between devices  15.5 us (1%)
  between operations  14.5 us (1%)
  loops' own time  12.3 us (1%)
    all_gather x1, blocking collectives, on_device(): block_rows = lax.all_gather(top_rows, 'grp', axis=0, tiled=True)  315 us
    all_gather x1, waiting for transfers between devices, on_device(): lax.all_gather(scaled_own, 'grp', axis=0, tiled=True)  139 us
    add x128, other arithmetic, advance(): matrix + (keep_odd[:, None] * keep_even[None, :] - keep_even[:, None] * k...  104 us
    dynamic_update_slice x128, local copies, waits for them, and re-layouts, advance(): lax.dynamic_update_slice(pivots, pivot[None], (step.astype(jnp.int32),))  86.2 us
    select_n x128, other arithmetic, advance(): lower_odd = jnp.where(keep, -col_even / pivot, zeros)  84.3 us
    dynamic_slice x128, local copies, waits for them, and re-layouts, advance(): pivot = lax.dynamic_index_in_dim(col_odd, first, 0, keepdims=False)  75.5 us
    all_gather x1, waiting for transfers between devices, on_device(): lax.all_gather(right_own, 'grp', axis=0, tiled=True)  69.9 us
    dot_general x36, matrix products, orbitals(): values = jnp.dot(hidden, w_out, precision=lax.Precision.HIGHEST)  66.7 us
  transfers between devices with their start and end apart: 3, of which 2 were waited for; matrix products, arithmetic and copies ran while one was open for 3% of the time, Pallas kernels for 0%

profile of v1, /device:TPU:6, one launch (start us, length us, event | category | flops | bytes accessed | tf_op | source)
XLA Modules:
  0.0 1188.3 jit_solution(8840530697932588268)
XLA Ops:
  11.7 15.4 %all-to-all-start = ((bf16[128,16,256]{2,1,0:T(8,128)(2,1)}), bf16[128,16,256]{2,1,0:T(8,128)(2,1)S(1)}, u32[]{:S(2)}, u32[]{:S(2)}) async-start(bf16[128,16,256]{2,1,0:T(8,128)(2,1)} %stack.18), calls=%async_computation | async-start | bytes 2097152 | tf_op jit(solution)/shard_map/all_to_all | solution.py:95
  27.3 6.6 broadcast_multiply_fusion
  33.9 13.2 %mul.191 = f32[256,256]{1,0:T(8,128)} reshape(f32[128,2,128,2]{3,2,1,0:T(8,128)} %broadcast_multiply_fusion) | data formatting | bytes 524288 | tf_op jit(solution)/shard_map/jit(kron)/mul | solution.py:125
  48.3 69.9 %all-gather.5.cloned.1.call-done = bf16[2048,256]{1,0:T(8,128)(2,1)} async-done(((bf16[16,256]{1,0:T(8,128)(2,1)}), bf16[2048,256]{1,0:T(8,128)(2,1)}) %all-gather.5.cloned.1.call-update) | async-done | bytes 1048592 | tf_op jit(solution)/shard_map/all_gather | solution.py:97
  118.1 8.0 gather_fusion.1
  126.2 7.5 gather_fusion
  135.2 64.1 %while.65 = (s32[]{:T(128)}, f32[16,14,128]{2,1,0:T(8,128)}, bf16[14,256]{1,0:T(8,128)(2,1)S(1)}, bf16[16,128,256]{2,1,0:T(8,128)(2,1)S(1)}, f32[256]{0:T(256)S(...) while((s32[]{:T(128)}, f32[16,14,128]{2,1,0:T(8,128)}, ...), condition=%wide.region_7.9_spmd, body=%wide.region_6.8_spmd.sunk | while | flops 245927424 | bytes 9699465 | solution.py:27
  200.3 2.8 while.63
  203.1 2.5 while.64
  205.7 315.5 %all-gather = f32[128,2,256]{2,1,0:T(2,128)S(1)} all-gather(f32[1,2,256]{2,1,0:T(2,128)S(1)} %fusion.53), channel_id=1, replica_groups=mesh['walker'=2,'grp'=128] {'grp'}, dimensions={0}, use_global_device_ids=true | all-gather | bytes 264192 | tf_op jit(solution)/shard_map/all_gather | solution.py:123
  521.4 121.4 %while.66 = (s32[]{:T(128)}, f32[16,128,14]{2,1,0:T(8,128)}, bf16[16,128,256]{2,1,0:T(8,128)(2,1)}, bf16[14,256]{1,0:T(8,128)(2,1)S(1)}, f32[256]{0:T(256)S(1)},...) while((s32[]{:T(128)}, f32[16,128,14]{2,1,0:T(8,128)}, ...), condition=%wide.region_9.11_spmd, body=%wide.region_8.10_spmd.sunk | while | flops 245927424 | bytes 11606153 | solution.py:35
  524.1 2.1 convolution_add_fusion.11
  526.2 2.0 fusion.110
  531.6 2.1 convolution_add_fusion.11
  533.8 2.0 fusion.110
  539.2 2.1 convolution_add_fusion.11
  541.4 2.0 fusion.110
  546.8 2.1 convolution_add_fusion.11
  549.0 2.0 fusion.110
  554.4 2.1 convolution_add_fusion.11
  556.5 2.0 fusion.110
  562.0 2.1 convolution_add_fusion.11
  564.1 2.0 fusion.110
  569.5 2.1 convolution_add_fusion.11
  571.7 2.0 fusion.110
  577.1 2.1 convolution_add_fusion.11
  579.3 2.0 fusion.110
  584.7 2.1 convolution_add_fusion.11
  586.9 2.0 fusion.110
  592.3 2.1 convolution_add_fusion.11
  594.4 2.0 fusion.110
  599.9 2.1 convolution_add_fusion.11
  602.0 2.0 fusion.110
  607.5 2.1 convolution_add_fusion.11
  609.6 2.0 fusion.110
  615.0 2.1 convolution_add_fusion.11
  617.2 2.0 fusion.110
  622.6 2.1 convolution_add_fusion.11
  624.8 2.0 fusion.110
  630.2 2.1 convolution_add_fusion.11
  632.3 2.0 fusion.110
  637.8 2.1 convolution_add_fusion.11
  639.9 2.0 fusion.110
  644.6 365.8 %while.68 = (s32[]{:T(128)}, f32[256,256]{0,1:T(8,128)S(1)}, f32[256,256]{0,1:T(8,128)S(1)}, f32[128]{0:T(128)S(1)}, s32[]{:T(128)}, /*index=5*/s32[]{:T(128)}, s32[]{:T(128)}, s32[]{:T(128)}, s32[]{:T(128)}, s32[]{:T(128)}) while((s32[]{:T(128)}, f32[256,256]{0,1:T(8,128)S(1)}, f32[256,256]{0,1:T(8,128)S(1)}, ...), condition=%wide.region_5.7_spmd.clone.clone, body=%wide.region_4.6_spmd.clone.clone.sunk | while | flops 331276 | bytes 548637 | solution.py:68
  1010.5 5.4 while.67
  1015.9 20.5 %custom-call.4 = f32[2,128,128]{1,2,0:T(8,128)S(1)} custom-call(f32[2,128,128]{2,1,0:T(8,128)} %get-tuple-element.340), custom_call_target="InvertDiagBlocksLowerTriangular" | custom-call | tf_op jit(solution)/shard_map/jit(_solve_triangular)/triangular_solve | solution.py:80
  1038.9 138.6 %all-gather.7.cloned.1.call-done = f32[128,14,256]{2,1,0:T(8,128)} async-done(((f32[1,14,256]{2,1,0:T(8,128)}), f32[128,14,256]{2,1,0:T(8,128)}) %all-gather.7.cloned.1.call-update) | async-done | bytes 1835024 | tf_op jit(solution)/shard_map/all_gather | solution.py:134
  1179.2 2.3 convolution_subtract_fusion
  (1545 shorter events, 497.8 us)
Async XLA Ops:
  7.2 0.9 copy-start
  7.2 20.1 %copy-start.9 = (f32[2,2]{1,0:T(2,128)S(1)}, f32[2,2]{1,0:T(2,128)}, u32[]{:S(2)}) copy-start(f32[2,2]{1,0:T(2,128)} %constant.221.clone) | copy-start | bytes 52
  7.2 20.0 %copy-start.10 = (f32[128]{0:T(128)S(1)}, f32[128]{0:T(128)}, u32[]{:S(2)}) copy-start(f32[128]{0:T(128)} %param.30) | copy-start | bytes 1540
  7.2 110.9 %all-gather.5.cloned.1.call-start = ((), (), s32[]{:S(2)}) async-start(), calls=%async_computation.1 | async-start | bytes 1056768 | tf_op jit(solution)/shard_map/all_gather | solution.py:97
  11.7 114.5 %all-to-all-start = ((bf16[128,16,256]{2,1,0:T(8,128)(2,1)}), bf16[128,16,256]{2,1,0:T(8,128)(2,1)S(1)}, u32[]{:S(2)}, u32[]{:S(2)}) async-start(bf16[128,16,256]{2,1,0:T(8,128)(2,1)} %stack.18), calls=%async_computation | async-start | bytes 2097152 | tf_op jit(solution)/shard_map/all_to_all | solution.py:95
  27.1 1150.5 %all-gather.7.cloned.1.call-start = ((), (), s32[]{:S(2)}) async-start(), calls=%async_computation.2 | async-start | bytes 2113536 | tf_op jit(solution)/shard_map/all_gather | solution.py:134
  33.9 14.3 %copy-start.7 = (s32[2048]{0:T(1024)S(1)}, s32[2048]{0:T(1024)}, u32[]{:S(2)}) copy-start(s32[2048]{0:T(1024)} %param.23) | copy-start | bytes 24580
  133.7 1.5 copy-start.1
  133.7 1.5 copy-start.4
  133.7 1.5 copy-start.5
  134.2 1.0 copy-start.2
  135.9 0.7 copy-start.12
  139.9 0.7 copy-start.12
  143.9 0.7 copy-start.12
  147.9 0.7 copy-start.12
  151.9 0.7 copy-start.12
  155.9 0.7 copy-start.12
  159.9 0.7 copy-start.12
  163.9 0.7 copy-start.12
  167.9 0.7 copy-start.12
  171.9 0.7 copy-start.12
  175.9 0.7 copy-start.12
  180.0 0.7 copy-start.12
  184.0 0.7 copy-start.12
  188.0 0.7 copy-start.12
  192.0 0.7 copy-start.12
  196.0 0.7 copy-start.12
  521.4 123.0 %copy-start.3 = (f32[256,256]{1,0:T(8,128)S(1)}, f32[256,256]{1,0:T(8,128)}, u32[]{:S(2)}) copy-start(f32[256,256]{1,0:T(8,128)} %mul.191) | copy-start | bytes 786436
  524.1 2.1 copy-start.14
  531.6 2.1 copy-start.14
  539.2 2.1 copy-start.14
  546.8 2.1 copy-start.14
  554.4 2.1 copy-start.14
  562.0 2.1 copy-start.14
  569.5 2.1 copy-start.14
  577.1 2.1 copy-start.14
  584.7 2.1 copy-start.14
  592.3 2.1 copy-start.14
  599.9 2.1 copy-start.14
  607.5 2.1 copy-start.14
  615.0 2.1 copy-start.14
  622.6 2.1 copy-start.14
  630.2 2.1 copy-start.14
  637.8 2.1 copy-start.14
  642.7 1.8 copy-start.11
  644.5 365.9 %copy-start.8 = (s32[256]{0:T(256)S(1)}, s32[256]{0:T(256)}, u32[]{:S(2)}) copy-start(s32[256]{0:T(256)} %iota_add_fusion) | copy-start | bytes 3076
  644.5 365.9 %copy-start.15 = (s32[2]{0:T(128)S(1)}, s32[2]{0:T(128)}, u32[]{:S(2)}) copy-start(s32[2]{0:T(128)} %iota_multiply_fusion) | copy-start | bytes 28
  1036.9 142.3 %copy-start.6 = (f32[14,256]{1,0:T(8,128)}, f32[14,256]{1,0:T(8,128)S(1)}, u32[]{:S(2)}) copy-start(f32[14,256]{1,0:T(8,128)S(1)} %fusion.50) | copy-start | bytes 43012
  (2 other events, 1.4 us)
Sparse Core Ops, SparseCore 0:
  12.0 106.1 all-gather.4
  1038.5 138.9 all-gather.6
